TPU v7x, 256 devices: a whole 4x4x8 slice. The times are simulated.
256 devices in a mesh: seq: 64 (over x, y_hi, z), head: 4 (over y_lo, core).
Axes of the slice: x: 4, y: 4 (y_hi: 2, y_lo: 2; y = y_hi * 2 + y_lo), z: 8, core: 2. Of those that a mesh axis runs over, the one named last changes fastest.
Arguments:
- tokens: bfloat16 [16384, 1024], P('seq'), may hold values from -6 to 6
- queries: bfloat16 [16384, 1024], P('seq', 'head'), may hold values from -8 to 8
- key_rows: bfloat16 [16384, 1024], P('seq', 'head'), may hold values from -8 to 8
- values: bfloat16 [16384, 1024], P('seq', 'head'), may hold values from -6 to 6
- ssm_input: bfloat16 [16384, 2048], P('seq', 'head'), may hold values from -6 to 6
- write_proj: bfloat16 [16384, 128], P('seq'), may hold values from -6 to 6
- read_proj: bfloat16 [16384, 128], P('seq'), may hold values from -6 to 6
- log_decay: float32 [32, 16384], P('head', 'seq'), may hold values from -1 to 0
- attn_project: bfloat16 [1024, 1024], P('head'), may hold values from -0.1875 to 0.1875
- ssm_project: bfloat16 [2048, 1024], P('head'), may hold values from -0.125 to 0.125
- gauss_project: bfloat16 [1024, 768], replicated, may hold values from -0.1875 to 0.1875
- tile_owner: int32 [16384], P('seq'), may hold values from 0 to 3, as said below
Outputs:
- block_out: bfloat16 [16384, 1024], P(('seq', 'head'))
- tile_rows: bfloat16 [64, 4, 4, 32, 768], P('seq', 'head')
Inputs may be any that keep to these rules, and one draw needn't show every extreme that they name: `tile_owner`: in each aligned group of 64 tokens no owner is named by more than 32 tokens; in every block of 256 tokens one owner is named by exactly 32 tokens of each of its groups.
All inputs are finite; a program needn't handle non-finite values.
Results may differ from a plain program's by a relative error of at most 0.023.
Values may be sent and summed in bfloat16 or wider, within the bound.
No kernel may reach another device: no remote copies, remote signals or barrier semaphores. Data moves between devices by JAX's collectives and lax.ppermute only.
A program may use at most 128 MiB of HBM per device.

v0:
```python
import math
import jax
import jax.numpy as jnp
from jax import lax
from jax.sharding import PartitionSpec as P

HDIM = 64


def entering_2(array, axis, combine, identity):
    devices, mine = (lax.axis_size(axis), lax.axis_index(axis))
    everything = jax.tree.map(
        lambda part, kind: lax.all_gather(part.astype(kind), axis),
        array,
        (jnp.bfloat16, jnp.bfloat16),
    )
    start = jax.tree.map(
        lambda part, zero: jnp.broadcast_to(jnp.asarray(zero, part.dtype), part.shape),
        array,
        identity,
    )

    def hop(k, before):
        reached = k < mine
        new = combine(
            before, jax.tree.map(lambda part, own: part[k].astype(own.dtype), everything, array)
        )
        return jax.tree.map(lambda a, b: jnp.where(reached, a, b), new, before)

    return lax.fori_loop(0, devices, hop, start)


def chain_pieces(ssm_input, write_proj, read_proj, log_decay):
    row_count = write_proj.shape[0]
    head_count = log_decay.shape[0]
    head_width = ssm_input.shape[1] // head_count
    cumulative = jnp.cumsum(log_decay, axis=1)
    inputs_heads = ssm_input.reshape(row_count, head_count, head_width)
    later_rows = lax.broadcasted_iota(jnp.int32, (row_count, row_count), 0)
    earlier_cols = lax.broadcasted_iota(jnp.int32, (row_count, row_count), 1)
    log_gaps = cumulative[:, :, None] - cumulative[:, None, :]
    decays = jnp.exp(jnp.where((later_rows >= earlier_cols)[None], log_gaps, -jnp.inf))
    cross_terms = jnp.dot(read_proj, write_proj.T, preferred_element_type=jnp.float32)
    mixing = (decays * cross_terms[None]).astype(jnp.bfloat16)
    inner_part = jnp.einsum(
        "hts,shp->thp", mixing, inputs_heads, preferred_element_type=jnp.float32
    )
    tail_decay = jnp.exp(cumulative[:, -1:] - cumulative)
    tail_inputs = (inputs_heads.astype(jnp.float32) * tail_decay.T[:, :, None]).astype(jnp.bfloat16)
    local_state = jnp.einsum(
        "sn,shp->hnp", write_proj, tail_inputs, preferred_element_type=jnp.float32
    )
    total_decay = jnp.exp(cumulative[:, -1])
    return (cumulative, inner_part, local_state, total_decay)


def chain_output(cumulative, inner_part, entering, read_proj):
    entering_low = entering.astype(jnp.bfloat16)
    outer_part = jnp.einsum(
        "tn,hnp->thp", read_proj, entering_low, preferred_element_type=jnp.float32
    )
    mixture = inner_part + outer_part * jnp.exp(cumulative).T[:, :, None]
    scaled = mixture * lax.rsqrt(jnp.mean(mixture * mixture, axis=2, keepdims=True) + 1e-05)
    return scaled.reshape(scaled.shape[0], -1).astype(jnp.bfloat16)


def combine_states(earlier, latter):
    decay_first, state_first = earlier
    decay_second, state_second = latter
    return (decay_first * decay_second, decay_second[:, None, None] * state_first + state_second)


def pass_states(local_state, total_decay):
    identity = (jnp.ones_like(total_decay), jnp.zeros_like(local_state))
    prefix = entering_2((total_decay, local_state), "seq", combine_states, identity)
    return prefix[1]


def fold_keys(query_heads, key_rows, values):
    row_count, head_count, head_width = query_heads.shape
    scale = 1.0 / math.sqrt(head_width)
    initial = (
        jnp.full((head_count, row_count), -jnp.inf, jnp.float32),
        jnp.zeros((head_count, row_count), jnp.float32),
        jnp.zeros((head_count, row_count, head_width), jnp.float32),
    )
    key_piece = lax.all_gather(key_rows, "seq", axis=0, tiled=True)
    value_piece = lax.all_gather(values, "seq", axis=0, tiled=True)
    piece_rows = key_piece.shape[0]
    block_rows = math.gcd(piece_rows, 1024)

    def one_step(block_index, carry_state):
        run_max, run_sum, accumulated = carry_state
        key_block = lax.dynamic_slice_in_dim(
            key_piece, block_index * block_rows, block_rows, 0
        ).reshape(block_rows, head_count, head_width)
        value_block = lax.dynamic_slice_in_dim(
            value_piece, block_index * block_rows, block_rows, 0
        ).reshape(block_rows, head_count, head_width)
        scores = (
            jnp.einsum("qhd,khd->hqk", query_heads, key_block, preferred_element_type=jnp.float32)
            * scale
        )
        new_max = jnp.maximum(run_max, jnp.max(scores, axis=2))
        shrink = jnp.exp(run_max - new_max)
        raised = jnp.exp(scores - new_max[:, :, None])
        run_sum = run_sum * shrink + jnp.sum(raised, axis=2)
        accumulated = accumulated * shrink[:, :, None] + jnp.einsum(
            "hqk,khd->hqd",
            raised.astype(jnp.bfloat16),
            value_block,
            preferred_element_type=jnp.float32,
        )
        return (new_max, run_sum, accumulated)

    run_max, run_sum, accumulated = lax.fori_loop(0, piece_rows // block_rows, one_step, initial)
    attended = accumulated / run_sum[:, :, None]
    return (
        attended.transpose(1, 0, 2).reshape(row_count, head_count * head_width).astype(jnp.bfloat16)
    )


def slot_rank(owners_here, owner_count, group_rows):
    row_count = owners_here.shape[0]
    one_hot = (owners_here[:, None] == jnp.arange(owner_count, dtype=jnp.int32)[None, :]).astype(
        jnp.bfloat16
    )
    later_rows = lax.broadcasted_iota(jnp.int32, (row_count, row_count), 0)
    earlier_cols = lax.broadcasted_iota(jnp.int32, (row_count, row_count), 1)
    before = (
        (earlier_cols < later_rows) & (later_rows // group_rows == earlier_cols // group_rows)
    ).astype(jnp.bfloat16)
    counted = jnp.dot(before, one_hot, preferred_element_type=jnp.float32)
    return jnp.sum(counted * one_hot.astype(jnp.float32), axis=1)


def per_device(
    tokens,
    queries,
    key_rows,
    values,
    ssm_input,
    write_proj,
    read_proj,
    log_decay,
    attn_project,
    ssm_project,
    gauss_project,
    tile_owner,
):
    row_count = queries.shape[0]
    head_count = queries.shape[1] // HDIM
    query_heads = queries.reshape(row_count, head_count, HDIM)
    attended = fold_keys(query_heads, key_rows, values)
    cumulative, inner_part, local_state, total_decay = chain_pieces(
        ssm_input, write_proj, read_proj, log_decay
    )
    entering = pass_states(local_state, total_decay)
    ssm_mix = chain_output(cumulative, inner_part, entering, read_proj)
    owner_count = lax.axis_size("head")
    own_index = lax.axis_index("head")
    sub_rows = row_count // owner_count
    capacity = sub_rows // 2
    width_out = gauss_project.shape[1]
    slot_count = owner_count * capacity
    slot_ids = jnp.arange(slot_count, dtype=jnp.float32)
    update = lax.psum_scatter(
        (
            jnp.dot(attended, attn_project, preferred_element_type=jnp.float32)
            + jnp.dot(ssm_mix, ssm_project, preferred_element_type=jnp.float32)
        ).astype(jnp.bfloat16),
        "head",
        scatter_dimension=0,
        tiled=True,
    ).astype(jnp.float32)
    own_tokens = lax.dynamic_slice_in_dim(tokens, own_index * sub_rows, sub_rows, 0)
    block_out = (own_tokens.astype(jnp.float32) + update).astype(jnp.bfloat16)
    gaussians = jnp.dot(block_out, gauss_project, preferred_element_type=jnp.float32).astype(
        jnp.bfloat16
    )
    owners_here = lax.dynamic_slice_in_dim(tile_owner, own_index * sub_rows, sub_rows, 0)
    slot_value = owners_here.astype(jnp.float32) * capacity + slot_rank(
        owners_here, owner_count, sub_rows
    )
    selector = (slot_ids[:, None] == slot_value[None, :]).astype(jnp.bfloat16)
    packed = jnp.dot(selector, gaussians, preferred_element_type=jnp.float32).astype(jnp.bfloat16)
    packed = packed.reshape(owner_count, capacity, width_out)
    received = lax.all_to_all(packed, "head", split_axis=0, concat_axis=0, tiled=True)
    tile_rows = received.reshape(1, 1, owner_count, capacity, width_out)
    return (block_out, tile_rows)


def solution(mesh):
    in_specs = (
        P("seq", None),
        P("seq", "head"),
        P("seq", "head"),
        P("seq", "head"),
        P("seq", "head"),
        P("seq", None),
        P("seq", None),
        P("head", "seq"),
        P("head", None),
        P("head", None),
        P(),
        P("seq"),
    )
    out_specs = (P(("seq", "head"), None), P("seq", "head", None, None, None))
    return jax.shard_map(
        per_device, mesh=mesh, in_specs=in_specs, out_specs=out_specs, check_vma=False
    )
```

profile of v0, /device:TPU:1, one launch (start us, length us, event | category | flops | bytes accessed | tf_op | source)
XLA Modules:
  0.0 632.4 jit_solution(15385614962645540333)
XLA Ops:
  7.2 1.4 reduce-window.6
  9.1 1.1 copy.44
  10.2 1.7 fusion.16
  12.0 1.7 copy.41
  13.8 1.7 copy.43
  16.4 1.3 dynamic-slice
  18.4 161.7 %all-reduce = bf16[512]{0:T(512)(128)(2,1)S(1)} all-reduce(bf16[512]{0:T(512)(128)(2,1)S(1)} %dynamic-update-slice), channel_id=2, replica_groups=mesh['seq'=64,'head'=4] {'seq'}, use_global_device_ids=true, to_apply=%add | all-reduce | flops 512 | bytes 2048
  182.3 82.8 %while.33 = (s32[]{:T(128)}, f32[8,128,64]{2,1,0:T(8,128)S(1)}, s32[]{:T(128)}, bf16[64,8]{1,0:T(8,128)(2,1)S(1)}, bf16[64,8,128,64]{2,3,1,0:T(8,128)(2,1)}, /*index=5*/s32[]{:T(128)}, s32[]{:T(128)}) while((s32[]{:T(128)}, f32[8,128,64]{2,1,0:T(8,128)S(1)}, s32[]{:T(128)}, bf16[64,8]{1,0:T(8,128)(2,1)S(1)}, ...), condition=%wide.region_7.8_spmd.clone, body=%wide.region_6.7_spmd.clone.sunk | while | flops 327692 | bytes 1179833 | solution.py:30
  265.4 2.3 multiply_reduce_fusion
  267.7 41.6 %all-gather.6.cloned.1.call-done = bf16[16384,256]{0,1:T(8,128)(2,1)} async-done(((bf16[256,256]{0,1:T(8,128)(2,1)}), bf16[16384,256]{0,1:T(8,128)(2,1)}) %all-gather.6.cloned.1.call-update) | async-done | bytes 8388624 | tf_op jit(solution)/shard_map/all_gather | solution.py:87
  309.3 148.9 %all-gather.8.cloned.1.call-done = bf16[16384,256]{0,1:T(8,128)(2,1)} async-done(((bf16[256,256]{0,1:T(8,128)(2,1)}), bf16[16384,256]{0,1:T(8,128)(2,1)}) %all-gather.8.cloned.1.call-update) | async-done | bytes 8388624 | tf_op jit(solution)/shard_map/all_gather | solution.py:88
  458.2 133.3 %while.32 = (s32[]{:T(128)}, f32[4,256]{1,0:T(4,128)S(1)}, f32[4,256]{1,0:T(4,128)S(1)}, f32[4,256,64]{1,2,0:T(8,128)S(1)}, bf16[16384,256]{0,1:T(8,128)(2,1)}, ...) while((s32[]{:T(128)}, f32[4,256]{1,0:T(4,128)S(1)}, ...), condition=%wide.region_3.0_spmd.clone, body=%wide.region_0.0_spmd.clone.sunk | while | flops 277025792 | bytes 33226948 | solution.py:116
  458.2 1.3 constant_dynamic-slice_fusion.5
  459.5 2.7 bitcast_reduce_fusion.2
  462.2 3.0 fusion.66
  466.5 1.3 constant_dynamic-slice_fusion.5
  467.8 2.7 bitcast_reduce_fusion.2
  470.5 3.0 fusion.66
  474.9 1.3 constant_dynamic-slice_fusion.5
  476.1 2.7 bitcast_reduce_fusion.2
  478.8 3.0 fusion.66
  483.2 1.3 constant_dynamic-slice_fusion.5
  484.5 2.7 bitcast_reduce_fusion.2
  487.2 3.0 fusion.66
  491.5 1.3 constant_dynamic-slice_fusion.5
  492.8 2.7 bitcast_reduce_fusion.2
  495.5 3.0 fusion.66
  499.9 1.3 constant_dynamic-slice_fusion.5
  501.1 2.7 bitcast_reduce_fusion.2
  503.8 3.0 fusion.66
  508.2 1.3 constant_dynamic-slice_fusion.5
  509.5 2.7 bitcast_reduce_fusion.2
  512.2 3.0 fusion.66
  516.5 1.3 constant_dynamic-slice_fusion.5
  517.8 2.7 bitcast_reduce_fusion.2
  520.5 3.0 fusion.66
  524.8 1.3 constant_dynamic-slice_fusion.5
  526.1 2.7 bitcast_reduce_fusion.2
  528.8 3.0 fusion.66
  533.2 1.3 constant_dynamic-slice_fusion.5
  534.4 2.7 bitcast_reduce_fusion.2
  537.1 3.0 fusion.66
  541.5 1.3 constant_dynamic-slice_fusion.5
  542.8 2.7 bitcast_reduce_fusion.2
  545.5 3.0 fusion.66
  549.8 1.3 constant_dynamic-slice_fusion.5
  551.1 2.7 bitcast_reduce_fusion.2
  553.8 3.0 fusion.66
  558.2 1.3 constant_dynamic-slice_fusion.5
  559.4 2.7 bitcast_reduce_fusion.2
  562.1 3.0 fusion.66
  566.5 1.3 constant_dynamic-slice_fusion.5
  567.8 2.7 bitcast_reduce_fusion.2
  570.5 3.0 fusion.66
  574.8 1.3 constant_dynamic-slice_fusion.5
  576.1 2.7 bitcast_reduce_fusion.2
  578.8 3.0 fusion.66
  583.1 1.3 constant_dynamic-slice_fusion.5
  584.4 2.7 bitcast_reduce_fusion.2
  587.1 3.0 fusion.66
  592.6 1.7 fusion.41
  594.3 1.1 fusion.13
  595.9 20.9 %reduce-scatter.2.cloned.1.call-done = bf16[64,1024]{1,0:T(8,128)(2,1)} async-done(((bf16[256,1024]{1,0:T(8,128)(2,1)}), bf16[64,1024]{1,0:T(8,128)(2,1)}) %reduce-scatter.2.cloned.1.call-update) | async-done | bytes 131088 | tf_op jit(solution)/shard_map/reduce_scatter | solution.py:167
  618.4 6.8 %all_to_all.5 = bf16[4,32,768]{2,1,0:T(8,128)(2,1)S(1)} all-to-all(bf16[4,32,768]{2,1,0:T(8,128)(2,1)S(1)} %bitcast.92), channel_id=1, replica_groups=mesh['seq'=64,'head'=4] {'head'}, dimensions={0} | all-to-all | bytes 393216 | tf_op jit(solution)/shard_map/all_to_all | solution.py:188
  (400 shorter events, 108.8 us)
Async XLA Ops:
  7.2 610.6 %copy-start = (bf16[1024,768]{1,0:T(8,128)(2,1)S(1)}, bf16[1024,768]{1,0:T(8,128)(2,1)}, u32[]{:S(2)}) copy-start(bf16[1024,768]{1,0:T(8,128)(2,1)} %param.26) | copy-start | bytes 4718596
  7.2 175.1 %all-gather.10.cloned.1.call-start = ((), (), s32[]{:S(2)}) async-start(), calls=%async_computation.5 | async-start | bytes 8519680 | tf_op jit(solution)/shard_map/all_gather | solution.py:13
  12.0 297.3 %all-gather.6.cloned.1.call-start = ((), (), s32[]{:S(2)}) async-start(), calls=%async_computation.2 | async-start | bytes 8519680 | tf_op jit(solution)/shard_map/all_gather | solution.py:87
  13.7 444.4 %all-gather.8.cloned.1.call-start = ((), (), s32[]{:S(2)}) async-start(), calls=%async_computation.3 | async-start | bytes 8519680 | tf_op jit(solution)/shard_map/all_gather | solution.py:88
  15.5 601.3 %reduce-scatter.2.cloned.1.call-start = ((), (), s32[]{:S(2)}) async-start(), calls=%async_computation.4 | async-start | bytes 655360 | tf_op jit(solution)/shard_map/reduce_scatter | solution.py:167
  182.3 82.8 %copy-start.4 = (bf16[256,128]{1,0:T(8,128)(2,1)S(1)}, bf16[256,128]{1,0:T(8,128)(2,1)}, u32[]{:S(2)}) copy-start(bf16[256,128]{1,0:T(8,128)(2,1)} %param.22) | copy-start | bytes 196612
  458.2 136.1 %copy-start.2 = (bf16[256,1024]{1,0:T(8,128)(2,1)S(1)}, bf16[256,1024]{1,0:T(8,128)(2,1)}, u32[]{:S(2)}) copy-start(bf16[256,1024]{1,0:T(8,128)(2,1)} %param.24) | copy-start | bytes 1572868
  462.2 3.4 copy-start.1
  470.5 3.4 copy-start.1
  478.8 3.4 copy-start.1
  487.2 3.4 copy-start.1
  495.5 3.4 copy-start.1
  503.8 3.4 copy-start.1
  512.2 3.4 copy-start.1
  520.5 3.4 copy-start.1
  528.8 3.4 copy-start.1
  537.1 3.4 copy-start.1
  545.5 3.4 copy-start.1
  553.8 3.4 copy-start.1
  562.1 3.4 copy-start.1
  570.5 3.4 copy-start.1
  578.8 3.4 copy-start.1
  587.1 3.4 copy-start.1
  591.5 4.0 copy-start.5
  617.8 8.1 %copy-start.3 = (bf16[64,1024]{1,0:T(8,128)(2,1)}, bf16[64,1024]{1,0:T(8,128)(2,1)S(1)}, u32[]{:S(2)}) copy-start(bf16[64,1024]{1,0:T(8,128)(2,1)S(1)} %add_convert_fusion) | copy-start | bytes 393220
Sparse Core Ops, SparseCore 0:
  12.2 148.4 all-gather.9
  164.8 144.4 all-gather.5
  312.7 145.3 all-gather.7
  595.6 21.1 reduce-scatter.1
where the time goes:
time: 634 us; the launch traced here: 632 us
  waiting for transfers between devices  211 us (33%)
  blocking collectives  168 us (26%)
  local copies, waits for them, and re-layouts  105 us (17%)
  matrix products  66 us (10%)
  other arithmetic  63.3 us (10%)
  between operations  14.5 us (2%)
    unnamed x1, blocking collectives  162 us
    all_gather x1, waiting for transfers between devices, fold_keys(): value_piece = lax.all_gather(values, 'seq', axis=0, tiled=True)  149 us
    dynamic_slice x128, local copies, waits for them, and re-layouts, hop(): part[k].astype(own.dtype)  70.3 us
    reduce_sum x16, other arithmetic, one_step(): run_sum = run_sum * shrink + jnp.sum(raised, axis=2)  48.5 us
    dot_general x16, matrix products, one_step(): jnp.einsum('qhd,khd->hqk', query_heads, key_block, preferred_element_type...  43.1 us
    all_gather x1, waiting for transfers between devices, fold_keys(): key_piece = lax.all_gather(key_rows, 'seq', axis=0, tiled=True)  41.6 us
    reduce_scatter x1, waiting for transfers between devices, per_device(): lax.psum_scatter((jnp.dot(attended, attn_project, preferred_element_type=...  20.9 us
    dynamic_slice x16, local copies, waits for them, and re-layouts, one_step(): lax.dynamic_slice_in_dim(value_piece, block_index * block_rows, block_row...  20.5 us
  transfers between devices with their start and end apart: 4, of which 3 were waited for; matrix products, arithmetic and copies ran while one was open for 14% of the time, Pallas kernels for 0%

commit v1 on v0

--- a/solution.py
+++ b/solution.py
@@ -3,6 +3,7 @@
 import jax.numpy as jnp
 from jax import lax
 from jax.sharding import PartitionSpec as P
+from jax.lax import all_to_all, psum
 
 HDIM = 64
 
@@ -85,7 +86,13 @@
         jnp.zeros((head_count, row_count, head_width), jnp.float32),
     )
     key_piece = lax.all_gather(key_rows, "seq", axis=0, tiled=True)
-    value_piece = lax.all_gather(values, "seq", axis=0, tiled=True)
+
+    def work_the_ports(shard_in):
+        current_arr = jnp.stack(psum(1, "seq") * [shard_in])
+        current_value = all_to_all(current_arr, "seq", concat_axis=0, split_axis=0)
+        return jnp.concatenate(current_value, axis=0)
+
+    value_piece = work_the_ports(values)
     piece_rows = key_piece.shape[0]
     block_rows = math.gcd(piece_rows, 1024)
 

time: 634 us -> 739 us (1.17)
  blocking collectives: 168 us -> 368 us
  waiting for transfers between devices: 211 us -> 40.9 us
  matrix products: 66 us -> 101 us
  local copies, waits for them, and re-layouts: 105 us -> 129 us
  starting transfers between devices: 0.16 us -> 15.6 us
    unnamed x1, blocking collectives: 162 us -> 362 us
    all_gather x1 -> x0, waiting for transfers between devices: 149 us -> none  [fold_keys(): value_piece = lax.all_gather(values, 'seq', axis=0, tiled=True)]
    all_gather x1, waiting for transfers between devices: 41.6 us -> 0.01 us  [fold_keys(): key_piece = lax.all_gather(key_rows, 'seq', axis=0, tiled=True)]
    dot_general x16, matrix products: 13.9 us -> 48.6 us  [one_step(): jnp.einsum('hqk,khd->hqd', raised.astype(jnp.bfloat16), value_block, pref...]
    reduce_scatter x1, waiting for transfers between devices: 20.9 us -> 40.8 us  [per_device(): lax.psum_scatter((jnp.dot(attended, attn_project, preferred_element_type=...]
    dynamic_slice x0 -> x16, local copies, waits for them, and re-layouts: none -> 17.3 us  [one_step(): lax.dynamic_slice_in_dim(key_piece, block_index * block_rows, block_rows, 0)]
    all_to_all x0 -> x1, starting transfers between devices: none -> 15.5 us  [work_the_ports(): current_value = all_to_all(current_arr, 'seq', concat_axis=0, split_axis=0)]
    all_to_all x0 -> x1, local copies, waits for them, and re-layouts: none -> 11.9 us  [work_the_ports(): current_value = all_to_all(current_arr, 'seq', concat_axis=0, split_axis=0)]
  transfers between devices with their start and end apart: 4 -> 4, of which waited for: 3 -> 1; matrix products, arithmetic and copies ran while one was open for 14% -> 14% of each run, Pallas kernels for 0% -> 0%
where the time goes in v1:
time: 739 us; the launch traced here: 734 us
  blocking collectives  368 us (50%)
  local copies, waits for them, and re-layouts  129 us (17%)
  matrix products  101 us (14%)
  other arithmetic  60.9 us (8%)
  waiting for transfers between devices  40.9 us (6%)
  starting transfers between devices  15.6 us (2%)
  between operations  14.6 us (2%)
    unnamed x1, blocking collectives  362 us
    dynamic_slice x128, local copies, waits for them, and re-layouts, hop(): part[k].astype(own.dtype)  70.1 us
    dot_general x16, matrix products, one_step(): jnp.einsum('hqk,khd->hqd', raised.astype(jnp.bfloat16), value_block, pref...  48.6 us
    reduce_sum x16, other arithmetic, one_step(): run_sum = run_sum * shrink + jnp.sum(raised, axis=2)  46.1 us
    dot_general x16, matrix products, one_step(): jnp.einsum('qhd,khd->hqk', query_heads, key_block, preferred_element_type...  43.1 us
    reduce_scatter x1, waiting for transfers between devices, per_device(): lax.psum_scatter((jnp.dot(attended, attn_project, preferred_element_type=...  40.8 us
    dynamic_slice x32, local copies, waits for them, and re-layouts, one_step(): lax.dynamic_slice_in_dim(value_piece, block_index * block_rows, block_row...  20.6 us
    dynamic_slice x16, local copies, waits for them, and re-layouts, one_step(): lax.dynamic_slice_in_dim(key_piece, block_index * block_rows, block_rows, 0)  17.3 us
  transfers between devices with their start and end apart: 4, of which 1 were waited for; matrix products, arithmetic and copies ran while one was open for 14% of the time, Pallas kernels for 0%

profile of v1, /device:TPU:1, one launch (start us, length us, event | category | flops | bytes accessed | tf_op | source)
XLA Modules:
  0.0 734.0 jit_solution(1324960553260437137)
XLA Ops:
  7.2 1.4 reduce-window.6
  9.1 1.1 copy.53
  10.2 1.7 fusion.16
  13.0 4.2 stack.2
  17.2 15.5 %all-to-all-start = ((bf16[64,256,256]{1,2,0:T(8,128)(2,1)}), bf16[64,256,256]{1,2,0:T(8,128)(2,1)}, u32[]{:S(2)}, u32[]{:S(2)}) async-start(bf16[64,256,256]{1,2,0:T(8,128)(2,1)} %stack.2), calls=%async_computation | async-start | bytes 16777216 | tf_op jit(solution)/shard_map/all_to_all | solution.py:92
  35.4 361.6 %all-reduce = bf16[512]{0:T(512)(128)(2,1)S(1)} all-reduce(bf16[512]{0:T(512)(128)(2,1)S(1)} %dynamic-update-slice), channel_id=2, replica_groups=mesh['seq'=64,'head'=4] {'seq'}, use_global_device_ids=true, to_apply=%add | all-reduce | flops 512 | bytes 2048
  398.0 11.9 %copy.51 = bf16[64,256,256]{2,1,0:T(8,128)(2,1)} copy(bf16[64,256,256]{1,2,0:T(8,128)(2,1)} %all-to-all-done) | data formatting | bytes 16777216 | tf_op jit(solution)/shard_map/all_to_all | solution.py:92
  409.9 82.6 %while.33 = (s32[]{:T(128)}, f32[8,128,64]{2,1,0:T(8,128)S(1)}, s32[]{:T(128)}, bf16[64,8]{1,0:T(8,128)(2,1)S(1)}, bf16[64,8,128,64]{2,3,1,0:T(8,128)(2,1)}, /*index=5*/s32[]{:T(128)}, s32[]{:T(128)}) while((s32[]{:T(128)}, f32[8,128,64]{2,1,0:T(8,128)S(1)}, s32[]{:T(128)}, bf16[64,8]{1,0:T(8,128)(2,1)S(1)}, ...), condition=%wide.region_7.8_spmd.clone, body=%wide.region_6.7_spmd.clone.sunk | while | flops 327692 | bytes 1179833 | solution.py:31
  492.8 2.3 multiply_reduce_fusion
  495.1 177.0 %while.32 = (s32[]{:T(128)}, f32[4,256]{1,0:T(4,128)S(1)}, f32[4,256]{1,0:T(4,128)S(1)}, f32[4,256,64]{1,2,0:T(8,128)S(1)}, bf16[16384,256]{0,1:T(8,128)(2,1)}, ...) while((s32[]{:T(128)}, f32[4,256]{1,0:T(4,128)S(1)}, ...), condition=%wide.region_3.0_spmd.clone, body=%wide.region_0.0_spmd.clone.sunk | while | flops 277025792 | bytes 17498288 | solution.py:123
  496.2 2.7 bitcast_reduce_fusion.2
  498.9 2.9 fusion.66
  503.1 3.0 fusion.68
  507.3 2.7 bitcast_reduce_fusion.2
  510.0 2.9 fusion.66
  514.2 3.0 fusion.68
  518.4 2.7 bitcast_reduce_fusion.2
  521.1 2.9 fusion.66
  525.3 3.0 fusion.68
  529.4 2.7 bitcast_reduce_fusion.2
  532.1 2.9 fusion.66
  536.3 3.0 fusion.68
  540.5 2.7 bitcast_reduce_fusion.2
  543.2 2.9 fusion.66
  547.4 3.0 fusion.68
  551.6 2.7 bitcast_reduce_fusion.2
  554.3 2.9 fusion.66
  558.5 3.0 fusion.68
  561.6 1.1 constant_dynamic-slice_fusion.6
  562.6 2.7 bitcast_reduce_fusion.2
  565.3 2.9 fusion.66
  569.5 3.0 fusion.68
  573.7 2.7 bitcast_reduce_fusion.2
  576.4 2.9 fusion.66
  580.6 3.0 fusion.68
  584.8 2.7 bitcast_reduce_fusion.2
  587.5 2.9 fusion.66
  591.7 3.0 fusion.68
  595.8 2.7 bitcast_reduce_fusion.2
  598.5 2.9 fusion.66
  602.7 3.0 fusion.68
  606.9 2.7 bitcast_reduce_fusion.2
  609.6 2.9 fusion.66
  613.8 3.0 fusion.68
  618.0 2.7 bitcast_reduce_fusion.2
  620.7 2.9 fusion.66
  624.9 3.0 fusion.68
  629.0 2.7 bitcast_reduce_fusion.2
  631.7 2.9 fusion.66
  635.9 3.0 fusion.68
  640.1 2.7 bitcast_reduce_fusion.2
  642.8 2.9 fusion.66
  647.0 3.0 fusion.68
  651.2 2.7 bitcast_reduce_fusion.2
  653.9 2.9 fusion.66
  658.1 3.0 fusion.68
  662.2 2.7 bitcast_reduce_fusion.2
  664.9 2.9 fusion.66
  669.1 3.0 fusion.68
  672.2 1.1 multiply_convert_fusion.2
  673.3 1.7 fusion.41
  675.0 2.2 fusion.13
  677.6 40.8 %reduce-scatter.2.cloned.1.call-done = bf16[64,1024]{1,0:T(8,128)(2,1)} async-done(((bf16[256,1024]{1,0:T(8,128)(2,1)}), bf16[64,1024]{1,0:T(8,128)(2,1)}) %reduce-scatter.2.cloned.1.call-update) | async-done | bytes 131088 | tf_op jit(solution)/shard_map/reduce_scatter | solution.py:174
  720.1 6.7 all_to_all.10
  (407 shorter events, 124.8 us)
Async XLA Ops:
  7.2 712.3 %copy-start = (bf16[1024,768]{1,0:T(8,128)(2,1)S(1)}, bf16[1024,768]{1,0:T(8,128)(2,1)}, u32[]{:S(2)}) copy-start(bf16[1024,768]{1,0:T(8,128)(2,1)} %param.26) | copy-start | bytes 4718596
  7.2 402.7 %all-gather.7.cloned.1.call-start = ((), (), s32[]{:S(2)}) async-start(), calls=%async_computation.5 | async-start | bytes 8519680 | tf_op jit(solution)/shard_map/all_gather | solution.py:14
  17.2 15.6 %copy-start.4 = (bf16[256,256]{1,0:T(8,128)(2,1)S(1)}, bf16[256,256]{1,0:T(8,128)(2,1)}, u32[]{:S(2)}) copy-start(bf16[256,256]{1,0:T(8,128)(2,1)} %param.18) | copy-start | bytes 393220
  17.2 16.5 %copy-start.7 = (u32[256]{0:T(256)S(1)}, u32[256]{0:T(256)}, u32[]{:S(2)}) copy-start(u32[256]{0:T(256)} %constant.128) | copy-start | bytes 3076
  17.2 379.8 %copy-start.5 = (bf16[256,256]{1,0:T(8,128)(2,1)S(1)}, bf16[256,256]{1,0:T(8,128)(2,1)}, u32[]{:S(2)}) copy-start(bf16[256,256]{1,0:T(8,128)(2,1)} %param.17) | copy-start | bytes 393220
  17.2 380.6 %copy-start.2 = (bf16[256,128]{1,0:T(8,128)(2,1)S(1)}, bf16[256,128]{1,0:T(8,128)(2,1)}, u32[]{:S(2)}) copy-start(bf16[256,128]{1,0:T(8,128)(2,1)} %param.21) | copy-start | bytes 196612
  17.2 380.6 %copy-start.3 = (bf16[256,128]{1,0:T(8,128)(2,1)S(1)}, bf16[256,128]{1,0:T(8,128)(2,1)}, u32[]{:S(2)}) copy-start(bf16[256,128]{1,0:T(8,128)(2,1)} %param.22) | copy-start | bytes 196612
  17.2 380.8 %all-to-all-start = ((bf16[64,256,256]{1,2,0:T(8,128)(2,1)}), bf16[64,256,256]{1,2,0:T(8,128)(2,1)}, u32[]{:S(2)}, u32[]{:S(2)}) async-start(bf16[64,256,256]{1,2,0:T(8,128)(2,1)} %stack.2), calls=%async_computation | async-start | bytes 16777216 | tf_op jit(solution)/shard_map/all_to_all | solution.py:92
  32.8 462.4 %all-gather.5.cloned.1.call-start = ((), (), s32[]{:S(2)}) async-start(), calls=%async_computation.3 | async-start | bytes 8519680 | tf_op jit(solution)/shard_map/all_gather | solution.py:88
  33.6 684.8 %reduce-scatter.2.cloned.1.call-start = ((), (), s32[]{:S(2)}) async-start(), calls=%async_computation.4 | async-start | bytes 655360 | tf_op jit(solution)/shard_map/reduce_scatter | solution.py:174
  672.2 5.0 copy-start.6
  719.4 8.0 %copy-start.1 = (bf16[64,1024]{1,0:T(8,128)(2,1)}, bf16[64,1024]{1,0:T(8,128)(2,1)S(1)}, u32[]{:S(2)}) copy-start(bf16[64,1024]{1,0:T(8,128)(2,1)S(1)} %add_convert_fusion) | copy-start | bytes 393220
Sparse Core Ops, SparseCore 0:
  12.2 240.0 all-gather.6
  256.4 145.6 all-gather.4
  677.3 41.0 reduce-scatter.1
